TPU v7x, 32 devices: a whole 2x2x4 slice. The times are simulated.
32 devices in a mesh: mem: 4 (over y, core), row: 8 (over z, x).
Axes of the slice: x: 2, y: 2, z: 4, core: 2. Of those that a mesh axis runs over, the one named last changes fastest.
Arguments:
- starting_states: float32 [8, 8, 64, 512], P('mem', None, 'row'), may hold values from -6 to 6
- wind_east: float32 [8, 64, 512], P(None, 'row'), may hold values from -0.25 to 0.25
- wind_north: float32 [8, 64, 512], P(None, 'row'), may hold values from -0.25 to 0.25
- diffusivity: float32 [8, 64, 512], P(None, 'row'), may hold values from 0.05 to 0.22
- embed_weight: bfloat16 [8, 64], replicated, may hold values from -2 to 2
- norm_gain: float32 [64], replicated, may hold values from 0.1 to 1.9
- project_weight: bfloat16 [64, 192], replicated, may hold values from -0.75 to 0.75
- head_scale: float32 [4], replicated, may hold values from 1 to 10
- output_weight: bfloat16 [64, 64], replicated, may hold values from -0.75 to 0.75
- readout_weight: bfloat16 [64, 8], replicated, may hold values from -0.75 to 0.75
- first_kernel: bfloat16 [9, 8, 8], replicated, may hold values from -0.75 to 0.75
- second_kernel: bfloat16 [9, 8, 8], replicated, may hold values from -0.75 to 0.75
Outputs:
- postprocessed: bfloat16 [8, 8, 64, 512], P(None, None, 'row', 'mem')
All inputs are finite; a program needn't handle non-finite values.
Results may differ from a plain program's by a relative error of at most 0.0096.
Values may be sent and summed in bfloat16 or wider, within the bound.
No kernel may reach another device: no remote copies, remote signals or barrier semaphores. Data moves between devices by JAX's collectives and lax.ppermute only.
A program may use at most 64 MiB of HBM per device.

v0:
```python
import jax
import jax.numpy as jnp
from jax import lax
from jax.sharding import PartitionSpec as P

STEPS = 4
DILATION_SPAN = 4


def padded(block, sides, width):
    for axis, dim in sides:
        count = lax.axis_size(axis)
        forward = [(i, i + 1) for i in range(count - 1)]
        backward = [(target, source) for source, target in forward]
        low = lax.ppermute(
            lax.slice_in_dim(block, block.shape[dim] - width, None, axis=dim), axis, forward
        )
        high = lax.ppermute(lax.slice_in_dim(block, 0, width, axis=dim), axis, backward)
        block = jnp.concatenate([low, block, high], axis=dim)
    return block


def advance(padded_field, wind_east, wind_north, diffusivity):
    middle = padded_field[..., 1:-1, :]
    northern = padded_field[..., 2:, :]
    southern = padded_field[..., :-2, :]
    widths = [(0, 0)] * (middle.ndim - 1) + [(1, 1)]
    widened = jnp.pad(middle, widths)
    eastern = widened[..., 2:]
    western = widened[..., :-2]
    drifting = 0.2 * jnp.tanh(middle)
    laplace = northern + southern + eastern + western - 4.0 * middle
    return (
        middle
        - (wind_east + drifting) * (eastern - western) * 0.5
        - (wind_north + drifting) * (northern - southern) * 0.5
        + diffusivity * laplace
    )


def post_block(
    vertical_layers,
    embed_weight,
    norm_gain,
    project_weight,
    head_scale,
    output_weight,
    readout_weight,
):
    members, _, points = vertical_layers.shape
    width = embed_weight.shape[1]
    heads = head_scale.shape[0]
    head_size = width // heads
    embedded = jnp.einsum(
        "mlp,le->pme", vertical_layers, embed_weight, preferred_element_type=jnp.float32
    )
    meansq = jnp.mean(embedded * embedded, axis=-1, keepdims=True)
    normed = (embedded * lax.rsqrt(meansq + 1e-05) * norm_gain).astype(jnp.bfloat16)
    projected = jnp.einsum(
        "pme,ef->pmf", normed, project_weight, preferred_element_type=jnp.float32
    )
    queries = projected[..., :width].reshape(points, members, heads, head_size)
    keys_all = projected[..., width : 2 * width].reshape(points, members, heads, head_size)
    values = (
        projected[..., 2 * width :].astype(jnp.bfloat16).reshape(points, members, heads, head_size)
    )
    queries = (queries * lax.rsqrt(jnp.sum(queries * queries, -1, keepdims=True) + 1.0)).astype(
        jnp.bfloat16
    )
    keys_all = (keys_all * lax.rsqrt(jnp.sum(keys_all * keys_all, -1, keepdims=True) + 1.0)).astype(
        jnp.bfloat16
    )
    scores = jnp.einsum("pmhd,pnhd->phmn", queries, keys_all, preferred_element_type=jnp.float32)
    scores = scores * head_scale[:, None, None]
    weights = jnp.exp(scores)
    probs = (weights / jnp.sum(weights, -1, keepdims=True)).astype(jnp.bfloat16)
    mixed = jnp.einsum("phmn,pnhd->pmhd", probs, values, preferred_element_type=jnp.float32)
    mixed = mixed.astype(jnp.bfloat16).reshape(points, members, width)
    attended = jnp.einsum("pme,ef->pmf", mixed, output_weight, preferred_element_type=jnp.float32)
    residual = (embedded + attended).astype(jnp.bfloat16)
    step_result = jnp.einsum(
        "pme,ef->mfp", residual, readout_weight, preferred_element_type=jnp.float32
    )
    return step_result.astype(jnp.bfloat16)


def convolve(padded_field, kernel):
    row_total = padded_field.shape[2] - 2 * DILATION_SPAN
    column_total = padded_field.shape[3] - 2 * DILATION_SPAN
    summed = jnp.zeros(
        (padded_field.shape[0], kernel.shape[1], row_total, column_total), jnp.float32
    )
    for row_stencil in range(3):
        for column_stencil in range(3):
            shifted_field = padded_field[
                :,
                :,
                row_stencil * DILATION_SPAN : row_stencil * DILATION_SPAN + row_total,
                column_stencil * DILATION_SPAN : column_stencil * DILATION_SPAN + column_total,
            ]
            summed = summed + jnp.einsum(
                "oc,mcij->moij",
                kernel[row_stencil * 3 + column_stencil],
                shifted_field,
                preferred_element_type=jnp.float32,
            )
    return summed


def on_device(
    starting_states,
    wind_east,
    wind_north,
    diffusivity,
    embed_weight,
    norm_gain,
    project_weight,
    head_scale,
    output_weight,
    readout_weight,
    first_kernel,
    second_kernel,
):
    members_here = starting_states.shape[0]
    row_total = starting_states.shape[2]
    coefficients = jnp.stack([wind_east, wind_north, diffusivity])
    joined = jnp.concatenate([starting_states, coefficients], 0)
    widened = padded(joined, (("row", 2),), STEPS)
    gridded_quantity_list = widened[:members_here]
    coef_rows = widened[members_here:]
    first_row = lax.axis_index("row") * row_total - STEPS
    all_rows = lax.axis_size("row") * row_total
    for section in range(STEPS):
        out_rows = row_total + 2 * (STEPS - section - 1)
        offset = section + 1
        window = coef_rows[:, :, offset : offset + out_rows]
        gridded_quantity_list = advance(gridded_quantity_list, window[0], window[1], window[2])
        row_ids = first_row + offset + jnp.arange(out_rows)
        inside = (row_ids >= 0) & (row_ids < all_rows)
        gridded_quantity_list = jnp.where(inside[None, None, :, None], gridded_quantity_list, 0.0)
    predicted_states = gridded_quantity_list.astype(jnp.bfloat16)
    blockwise_quantity = lax.all_to_all(
        predicted_states, "mem", split_axis=3, concat_axis=0, tiled=True
    )
    members, levels_count, tile_rows, tile_cols = blockwise_quantity.shape
    count = tile_rows * tile_cols
    flattened = blockwise_quantity.reshape(members, levels_count, count)
    block = 256

    def one_block(block_index):
        vertical_layers = lax.dynamic_slice_in_dim(flattened, block_index * block, block, 2)
        return post_block(
            vertical_layers,
            embed_weight,
            norm_gain,
            project_weight,
            head_scale,
            output_weight,
            readout_weight,
        )

    blocks = lax.map(one_block, jnp.arange(count // block))
    step_result = jnp.moveaxis(blocks, 0, 2)
    features = step_result.reshape(members, readout_weight.shape[1], tile_rows, tile_cols)
    tile_cols = features.shape[3]
    padded_feature = padded(features, (("mem", 3), ("row", 2)), DILATION_SPAN)
    interior_cells = jax.nn.silu(convolve(padded_feature, first_kernel)).astype(jnp.bfloat16)
    activated_output = padded(interior_cells, (("mem", 3), ("row", 2)), DILATION_SPAN)
    return (features.astype(jnp.float32) + convolve(activated_output, second_kernel)).astype(
        jnp.bfloat16
    )


def solution(mesh):
    return jax.shard_map(
        on_device,
        mesh=mesh,
        in_specs=(
            P("mem", None, "row", None),
            P(None, "row", None),
            P(None, "row", None),
            P(None, "row", None),
            P(),
            P(),
            P(),
            P(),
            P(),
            P(),
            P(),
            P(),
        ),
        out_specs=P(None, None, "row", "mem"),
        check_vma=False,
    )
```

profile of v0, /device:TPU:1, one launch (start us, length us, event | category | flops | bytes accessed | tf_op | source)
XLA Modules:
  0.0 220.1 jit_solution(953675717168693512)
XLA Ops:
  0.0 1.0 copy.200
  1.0 1.1 copy.121
  2.1 1.1 fusion.90
  3.4 4.0 %collective-permute-start = (f32[5,8,4,512]{3,1,2,0:T(8,128)S(1)}, f32[5,8,4,512]{3,1,2,0:T(8,128)S(1)}, u32[]{:S(2)}, u32[]{:S(2)}) collective-permute-start(f32[5,8,4,512]{3,1,2,0:T(8,128)S(1)} %get-tuple-element.115), channel_id=1, source_target_pairs={{0,1},{1,2},{2,3},{3,4},{4,5},{5,6},{6,7},{8,9},{9,10},{10,11},{11... | collective-permute-start | bytes 983048 | tf_op jit(solution)/shard_map/ppermute | solution.py:15
  7.3 1.3 collective-permute-start.1
  8.8 11.9 %collective-permute-done = f32[5,8,4,512]{3,1,2,0:T(8,128)S(1)} collective-permute-done((f32[5,8,4,512]{3,1,2,0:T(8,128)S(1)}, f32[5,8,4,512]{3,1,2,0:T(8,128)S(1)}, u32[]{:S(2)}, u32[]{:S(2)}) %collective-permute-start) | collective-permute-done | bytes 327712 | tf_op jit(solution)/shard_map/ppermute | solution.py:15
  21.0 0.5 add_select_fusion
  22.7 2.0 copy.125
  24.7 2.8 %reshape.99 = bf16[4,2,8192]{2,1,0:T(2,128)(2,1)} reshape(bf16[512,2,8,8]{3,2,1,0:T(8,128)(2,1)S(1)} %bitcast.241) | data formatting | bytes 262144
  27.6 4.8 %all-to-all-start = ((bf16[4,2,8192]{2,1,0:T(2,128)(2,1)}), bf16[4,2,8192]{2,1,0:T(2,128)(2,1)S(1)}, u32[]{:S(2)}, u32[]{:S(2)}) async-start(bf16[4,2,8192]{2,1,0:T(2,128)(2,1)} %reshape.99), calls=%async_computation | async-start | bytes 262144 | tf_op jit(solution)/shard_map/all_to_all | solution.py:142
  35.1 0.9 all-to-all-done
  36.0 2.4 %reshape.100 = bf16[512,2,8,8]{3,2,1,0:T(8,128)(2,1)S(1)} reshape(bf16[4,2,8192]{2,1,0:T(2,128)(2,1)S(1)} %all-to-all-done) | data formatting | bytes 262144
  38.4 1.7 copy.126
  40.2 135.4 %while.10 = (s32[]{:T(128)}, bf16[4,8,8,256]{3,2,1,0:T(8,128)(2,1)S(1)}, s32[4]{0:T(128)S(1)}, bf16[8,8,1024]{2,1,0:T(8,128)(2,1)S(1)}, bf16[8,64]{1,0:T(8,128)(...) while((s32[]{:T(128)}, ...), condition=%wide.region_5.6_spmd, body=%wide.region_0.5_spmd.sunk | while | flops 77932544 | bytes 12530179 | solution.py:162
  40.4 0.6 dynamic_slice.14
  42.8 3.7 %copy.208 = bf16[256,8,4,16]{3,1,2,0:T(8,128)(2,1)} copy(bf16[256,8,4,16]{0,3,2,1:T(8,128)(2,1)S(1)} %get-tuple-element.230) | data formatting | bytes 524288 | tf_op jit(solution)/shard_map/while/body/eval_jaxpr/convert_element_type | solution.py:67
  46.5 3.8 %copy.209 = bf16[256,8,4,16]{3,1,2,0:T(8,128)(2,1)} copy(bf16[256,8,4,16]{0,3,2,1:T(8,128)(2,1)S(1)} %get-tuple-element.231) | data formatting | bytes 524288 | tf_op jit(solution)/shard_map/while/body/eval_jaxpr/convert_element_type | solution.py:70
  50.3 5.4 %fusion.123 = f32[256,4,8,8]{2,3,1,0:T(8,128)} fusion(bf16[256,8,4,16]{3,1,2,0:T(8,128)(2,1)} %copy.208, bf16[256,8,4,16]{3,1,2,0:T(8,128)(2,1)} %copy.209), kind=kOutput, calls=%fused_computation.154.clone.1 | convolution fusion | flops 2097152 | bytes 786432 | tf_op jit(solution)/shard_map/while/body/eval_jaxpr/pmhd,pnhd->phmn/dot_general | solution.py:73
  55.7 3.6 %copy.210 = f32[256,4,8,8]{0,3,2,1:T(8,128)S(1)} copy(f32[256,4,8,8]{2,3,1,0:T(8,128)} %fusion.123) | data formatting | bytes 524288 | tf_op jit(solution)/shard_map/while/body/eval_jaxpr/pmhd,pnhd->phmn/dot_general | solution.py:73
  59.6 3.7 %copy.211 = bf16[256,4,8,8]{3,2,1,0:T(8,128)(2,1)} copy(bf16[256,4,8,8]{0,3,2,1:T(8,128)(2,1)S(1)} %divide_convert_fusion.2) | data formatting | bytes 262144 | tf_op jit(solution)/shard_map/while/body/eval_jaxpr/convert_element_type | solution.py:76
  63.2 3.7 %copy.207 = bf16[256,8,4,16]{3,1,2,0:T(8,128)(2,1)} copy(bf16[256,8,4,16]{0,3,2,1:T(8,128)(2,1)S(1)} %bitcast.240) | data formatting | bytes 524288 | tf_op jit(solution)/shard_map/while/body/eval_jaxpr/reshape | solution.py:65
  66.9 4.1 %convert_bitcast_fusion.2 = bf16[256,8,4,16]{3,1,2,0:T(8,128)(2,1)} fusion(bf16[256,8,4,16]{3,1,2,0:T(8,128)(2,1)} %copy.207, bf16[256,4,8,8]{3,2,1,0:T(8,128)(2,1)S(1)} %copy-done), kind=kOutput, calls=%fused_computation.clone.1 | convolution fusion | flops 2228224 | bytes 655360 | tf_op jit(solution)/shard_map/while/body/eval_jaxpr/phmn,pnhd->pmhd/dot_general | solution.py:77
  71.1 2.7 %copy.212 = bf16[256,8,4,16]{0,3,2,1:T(8,128)(2,1)S(1)} copy(bf16[256,8,4,16]{3,1,2,0:T(8,128)(2,1)} %convert_bitcast_fusion.2) | data formatting | bytes 524288 | tf_op jit(solution)/shard_map/while/body/eval_jaxpr/convert_element_type | solution.py:78
  74.1 0.6 dynamic_slice.14
  76.6 3.7 %copy.208 = bf16[256,8,4,16]{3,1,2,0:T(8,128)(2,1)} copy(bf16[256,8,4,16]{0,3,2,1:T(8,128)(2,1)S(1)} %get-tuple-element.230) | data formatting | bytes 524288 | tf_op jit(solution)/shard_map/while/body/eval_jaxpr/convert_element_type | solution.py:67
  80.3 3.8 %copy.209 = bf16[256,8,4,16]{3,1,2,0:T(8,128)(2,1)} copy(bf16[256,8,4,16]{0,3,2,1:T(8,128)(2,1)S(1)} %get-tuple-element.231) | data formatting | bytes 524288 | tf_op jit(solution)/shard_map/while/body/eval_jaxpr/convert_element_type | solution.py:70
  84.1 5.4 %fusion.123 = f32[256,4,8,8]{2,3,1,0:T(8,128)} fusion(bf16[256,8,4,16]{3,1,2,0:T(8,128)(2,1)} %copy.208, bf16[256,8,4,16]{3,1,2,0:T(8,128)(2,1)} %copy.209), kind=kOutput, calls=%fused_computation.154.clone.1 | convolution fusion | flops 2097152 | bytes 786432 | tf_op jit(solution)/shard_map/while/body/eval_jaxpr/pmhd,pnhd->phmn/dot_general | solution.py:73
  89.5 3.6 %copy.210 = f32[256,4,8,8]{0,3,2,1:T(8,128)S(1)} copy(f32[256,4,8,8]{2,3,1,0:T(8,128)} %fusion.123) | data formatting | bytes 524288 | tf_op jit(solution)/shard_map/while/body/eval_jaxpr/pmhd,pnhd->phmn/dot_general | solution.py:73
  93.3 3.7 %copy.211 = bf16[256,4,8,8]{3,2,1,0:T(8,128)(2,1)} copy(bf16[256,4,8,8]{0,3,2,1:T(8,128)(2,1)S(1)} %divide_convert_fusion.2) | data formatting | bytes 262144 | tf_op jit(solution)/shard_map/while/body/eval_jaxpr/convert_element_type | solution.py:76
  97.0 3.7 %copy.207 = bf16[256,8,4,16]{3,1,2,0:T(8,128)(2,1)} copy(bf16[256,8,4,16]{0,3,2,1:T(8,128)(2,1)S(1)} %bitcast.240) | data formatting | bytes 524288 | tf_op jit(solution)/shard_map/while/body/eval_jaxpr/reshape | solution.py:65
  100.7 4.1 %convert_bitcast_fusion.2 = bf16[256,8,4,16]{3,1,2,0:T(8,128)(2,1)} fusion(bf16[256,8,4,16]{3,1,2,0:T(8,128)(2,1)} %copy.207, bf16[256,4,8,8]{3,2,1,0:T(8,128)(2,1)S(1)} %copy-done), kind=kOutput, calls=%fused_computation.clone.1 | convolution fusion | flops 2228224 | bytes 655360 | tf_op jit(solution)/shard_map/while/body/eval_jaxpr/phmn,pnhd->pmhd/dot_general | solution.py:77
  104.9 2.7 %copy.212 = bf16[256,8,4,16]{0,3,2,1:T(8,128)(2,1)S(1)} copy(bf16[256,8,4,16]{3,1,2,0:T(8,128)(2,1)} %convert_bitcast_fusion.2) | data formatting | bytes 524288 | tf_op jit(solution)/shard_map/while/body/eval_jaxpr/convert_element_type | solution.py:78
  107.9 0.6 dynamic_slice.14
  110.4 3.7 %copy.208 = bf16[256,8,4,16]{3,1,2,0:T(8,128)(2,1)} copy(bf16[256,8,4,16]{0,3,2,1:T(8,128)(2,1)S(1)} %get-tuple-element.230) | data formatting | bytes 524288 | tf_op jit(solution)/shard_map/while/body/eval_jaxpr/convert_element_type | solution.py:67
  114.1 3.8 %copy.209 = bf16[256,8,4,16]{3,1,2,0:T(8,128)(2,1)} copy(bf16[256,8,4,16]{0,3,2,1:T(8,128)(2,1)S(1)} %get-tuple-element.231) | data formatting | bytes 524288 | tf_op jit(solution)/shard_map/while/body/eval_jaxpr/convert_element_type | solution.py:70
  117.9 5.4 %fusion.123 = f32[256,4,8,8]{2,3,1,0:T(8,128)} fusion(bf16[256,8,4,16]{3,1,2,0:T(8,128)(2,1)} %copy.208, bf16[256,8,4,16]{3,1,2,0:T(8,128)(2,1)} %copy.209), kind=kOutput, calls=%fused_computation.154.clone.1 | convolution fusion | flops 2097152 | bytes 786432 | tf_op jit(solution)/shard_map/while/body/eval_jaxpr/pmhd,pnhd->phmn/dot_general | solution.py:73
  123.3 3.6 %copy.210 = f32[256,4,8,8]{0,3,2,1:T(8,128)S(1)} copy(f32[256,4,8,8]{2,3,1,0:T(8,128)} %fusion.123) | data formatting | bytes 524288 | tf_op jit(solution)/shard_map/while/body/eval_jaxpr/pmhd,pnhd->phmn/dot_general | solution.py:73
  127.1 3.7 %copy.211 = bf16[256,4,8,8]{3,2,1,0:T(8,128)(2,1)} copy(bf16[256,4,8,8]{0,3,2,1:T(8,128)(2,1)S(1)} %divide_convert_fusion.2) | data formatting | bytes 262144 | tf_op jit(solution)/shard_map/while/body/eval_jaxpr/convert_element_type | solution.py:76
  130.8 3.7 %copy.207 = bf16[256,8,4,16]{3,1,2,0:T(8,128)(2,1)} copy(bf16[256,8,4,16]{0,3,2,1:T(8,128)(2,1)S(1)} %bitcast.240) | data formatting | bytes 524288 | tf_op jit(solution)/shard_map/while/body/eval_jaxpr/reshape | solution.py:65
  134.5 4.1 %convert_bitcast_fusion.2 = bf16[256,8,4,16]{3,1,2,0:T(8,128)(2,1)} fusion(bf16[256,8,4,16]{3,1,2,0:T(8,128)(2,1)} %copy.207, bf16[256,4,8,8]{3,2,1,0:T(8,128)(2,1)S(1)} %copy-done), kind=kOutput, calls=%fused_computation.clone.1 | convolution fusion | flops 2228224 | bytes 655360 | tf_op jit(solution)/shard_map/while/body/eval_jaxpr/phmn,pnhd->pmhd/dot_general | solution.py:77
  138.6 2.7 %copy.212 = bf16[256,8,4,16]{0,3,2,1:T(8,128)(2,1)S(1)} copy(bf16[256,8,4,16]{3,1,2,0:T(8,128)(2,1)} %convert_bitcast_fusion.2) | data formatting | bytes 524288 | tf_op jit(solution)/shard_map/while/body/eval_jaxpr/convert_element_type | solution.py:78
  141.7 0.6 dynamic_slice.14
  144.1 3.7 %copy.208 = bf16[256,8,4,16]{3,1,2,0:T(8,128)(2,1)} copy(bf16[256,8,4,16]{0,3,2,1:T(8,128)(2,1)S(1)} %get-tuple-element.230) | data formatting | bytes 524288 | tf_op jit(solution)/shard_map/while/body/eval_jaxpr/convert_element_type | solution.py:67
  147.9 3.8 %copy.209 = bf16[256,8,4,16]{3,1,2,0:T(8,128)(2,1)} copy(bf16[256,8,4,16]{0,3,2,1:T(8,128)(2,1)S(1)} %get-tuple-element.231) | data formatting | bytes 524288 | tf_op jit(solution)/shard_map/while/body/eval_jaxpr/convert_element_type | solution.py:70
  151.7 5.4 %fusion.123 = f32[256,4,8,8]{2,3,1,0:T(8,128)} fusion(bf16[256,8,4,16]{3,1,2,0:T(8,128)(2,1)} %copy.208, bf16[256,8,4,16]{3,1,2,0:T(8,128)(2,1)} %copy.209), kind=kOutput, calls=%fused_computation.154.clone.1 | convolution fusion | flops 2097152 | bytes 786432 | tf_op jit(solution)/shard_map/while/body/eval_jaxpr/pmhd,pnhd->phmn/dot_general | solution.py:73
  157.1 3.6 %copy.210 = f32[256,4,8,8]{0,3,2,1:T(8,128)S(1)} copy(f32[256,4,8,8]{2,3,1,0:T(8,128)} %fusion.123) | data formatting | bytes 524288 | tf_op jit(solution)/shard_map/while/body/eval_jaxpr/pmhd,pnhd->phmn/dot_general | solution.py:73
  160.9 3.7 %copy.211 = bf16[256,4,8,8]{3,2,1,0:T(8,128)(2,1)} copy(bf16[256,4,8,8]{0,3,2,1:T(8,128)(2,1)S(1)} %divide_convert_fusion.2) | data formatting | bytes 262144 | tf_op jit(solution)/shard_map/while/body/eval_jaxpr/convert_element_type | solution.py:76
  164.6 3.7 %copy.207 = bf16[256,8,4,16]{3,1,2,0:T(8,128)(2,1)} copy(bf16[256,8,4,16]{0,3,2,1:T(8,128)(2,1)S(1)} %bitcast.240) | data formatting | bytes 524288 | tf_op jit(solution)/shard_map/while/body/eval_jaxpr/reshape | solution.py:65
  168.3 4.1 %convert_bitcast_fusion.2 = bf16[256,8,4,16]{3,1,2,0:T(8,128)(2,1)} fusion(bf16[256,8,4,16]{3,1,2,0:T(8,128)(2,1)} %copy.207, bf16[256,4,8,8]{3,2,1,0:T(8,128)(2,1)S(1)} %copy-done), kind=kOutput, calls=%fused_computation.clone.1 | convolution fusion | flops 2228224 | bytes 655360 | tf_op jit(solution)/shard_map/while/body/eval_jaxpr/phmn,pnhd->pmhd/dot_general | solution.py:77
  172.4 2.7 %copy.212 = bf16[256,8,4,16]{0,3,2,1:T(8,128)(2,1)S(1)} copy(bf16[256,8,4,16]{3,1,2,0:T(8,128)(2,1)} %convert_bitcast_fusion.2) | data formatting | bytes 524288 | tf_op jit(solution)/shard_map/while/body/eval_jaxpr/convert_element_type | solution.py:78
  175.8 2.9 %collective-permute-start.2 = (bf16[8,8,8,4]{3,1,2,0:T(8,128)(2,1)S(1)}, bf16[8,8,8,4]{3,1,2,0:T(8,128)(2,1)S(1)}, u32[]{:S(2)}, u32[]{:S(2)}) collective-permute-start(bf16[8,8,8,4]{3,1,2,0:T(8,128)(2,1)S(1)} %get-tuple-element.127), channel_id=1, source_target_pairs={{0,8},{8,16},{16,24},{1,9},{9,17},{17,25},{2,10},{10,18},{18,26},{... | collective-permute-start | bytes 12296 | tf_op jit(solution)/shard_map/ppermute | solution.py:15
  178.8 1.9 collective-permute-start.3
  180.9 4.2 %collective-permute-done.3 = bf16[8,8,8,4]{3,1,2,0:T(8,128)(2,1)S(1)} collective-permute-done((bf16[8,8,8,4]{3,1,2,0:T(8,128)(2,1)S(1)}, bf16[8,8,8,4]{3,1,2,0:T(8,128)(2,1)S(1)}, u32[]{:S(2)}, u32[]{:S(2)}) %collective-permute-start.3) | collective-permute-done | bytes 4128 | tf_op jit(solution)/shard_map/ppermute | solution.py:18
  185.3 4.1 %collective-permute-start.4 = (bf16[8,8,4,136]{3,1,2,0:T(8,128)(2,1)S(1)}, bf16[8,8,4,136]{3,1,2,0:T(8,128)(2,1)S(1)}, u32[]{:S(2)}, u32[]{:S(2)}) collective-permute-start(bf16[8,8,4,136]{3,1,2,0:T(8,128)(2,1)S(1)} %get-tuple-element.123), channel_id=1, source_target_pairs={{0,1},{1,2},{2,3},{3,4},{4,5},{5,6},{6,7},{8,9},{9,10},{10,11},{11... | collective-permute-start | bytes 208904 | tf_op jit(solution)/shard_map/ppermute | solution.py:15
  189.4 1.5 collective-permute-start.5
  191.3 4.5 %collective-permute-done.5 = bf16[8,8,4,136]{3,1,2,0:T(8,128)(2,1)S(1)} collective-permute-done((bf16[8,8,4,136]{3,1,2,0:T(8,128)(2,1)S(1)}, bf16[8,8,4,136]{3,1,2,0:T(8,128)(2,1)S(1)}, u32[]{:S(2)}, u32[]{:S(2)}) %collective-permute-start.5) | collective-permute-done | bytes 69664 | tf_op jit(solution)/shard_map/ppermute | solution.py:18
  197.9 2.9 %collective-permute-start.6 = (bf16[8,8,8,4]{3,1,2,0:T(8,128)(2,1)S(1)}, bf16[8,8,8,4]{3,1,2,0:T(8,128)(2,1)S(1)}, u32[]{:S(2)}, u32[]{:S(2)}) collective-permute-start(bf16[8,8,8,4]{3,1,2,0:T(8,128)(2,1)S(1)} %get-tuple-element.125), channel_id=1, source_target_pairs={{0,8},{8,16},{16,24},{1,9},{9,17},{17,25},{2,10},{10,18},{18,26},{... | collective-permute-start | bytes 12296 | tf_op jit(solution)/shard_map/ppermute | solution.py:15
  200.8 1.9 collective-permute-start.7
  202.9 4.2 %collective-permute-done.7 = bf16[8,8,8,4]{3,1,2,0:T(8,128)(2,1)S(1)} collective-permute-done((bf16[8,8,8,4]{3,1,2,0:T(8,128)(2,1)S(1)}, bf16[8,8,8,4]{3,1,2,0:T(8,128)(2,1)S(1)}, u32[]{:S(2)}, u32[]{:S(2)}) %collective-permute-start.7) | collective-permute-done | bytes 4128 | tf_op jit(solution)/shard_map/ppermute | solution.py:18
  207.3 4.5 %collective-permute-start.8 = (bf16[8,8,4,136]{3,1,2,0:T(8,128)(2,1)S(1)}, bf16[8,8,4,136]{3,1,2,0:T(8,128)(2,1)S(1)}, u32[]{:S(2)}, u32[]{:S(2)}) collective-permute-start(bf16[8,8,4,136]{3,1,2,0:T(8,128)(2,1)S(1)} %get-tuple-element.121), channel_id=1, source_target_pairs={{0,1},{1,2},{2,3},{3,4},{4,5},{5,6},{6,7},{8,9},{9,10},{10,11},{11... | collective-permute-start | bytes 208904 | tf_op jit(solution)/shard_map/ppermute | solution.py:15
  211.9 1.3 collective-permute-start.9
  213.4 1.8 collective-permute-done.8
  215.1 2.4 %collective-permute-done.9 = bf16[8,8,4,136]{3,1,2,0:T(8,128)(2,1)S(1)} collective-permute-done((bf16[8,8,4,136]{3,1,2,0:T(8,128)(2,1)S(1)}, bf16[8,8,4,136]{3,1,2,0:T(8,128)(2,1)S(1)}, u32[]{:S(2)}, u32[]{:S(2)}) %collective-permute-start.9) | collective-permute-done | bytes 69664 | tf_op jit(solution)/shard_map/ppermute | solution.py:18
  219.5 0.7 copy.154
  (137 shorter events, 16.9 us)
Async XLA Ops:
  0.0 8.7 %copy-start.1 = (bf16[9,8,8]{0,2,1:T(8,128)(2,1)S(1)}, bf16[9,8,8]{0,2,1:T(8,128)(2,1)}, u32[]{:S(2)}) copy-start(bf16[9,8,8]{0,2,1:T(8,128)(2,1)} %param.24) | copy-start | bytes 3460
  3.4 17.3 %collective-permute-start = (f32[5,8,4,512]{3,1,2,0:T(8,128)S(1)}, f32[5,8,4,512]{3,1,2,0:T(8,128)S(1)}, u32[]{:S(2)}, u32[]{:S(2)}) collective-permute-start(f32[5,8,4,512]{3,1,2,0:T(8,128)S(1)} %get-tuple-element.115), channel_id=1, source_target_pairs={{0,1},{1,2},{2,3},{3,4},{4,5},{5,6},{6,7},{8,9},{9,10},{10,11},{11... | collective-permute-start | bytes 983048 | tf_op jit(solution)/shard_map/ppermute | solution.py:15
  7.3 13.4 %collective-permute-start.1 = (f32[5,8,4,512]{3,1,2,0:T(8,128)S(1)}, f32[5,8,4,512]{3,1,2,0:T(8,128)S(1)}, u32[]{:S(2)}, u32[]{:S(2)}) collective-permute-start(f32[5,8,4,512]{3,1,2,0:T(8,128)S(1)} %get-tuple-element.116), channel_id=1, source_target_pairs={{1,0},{2,1},{3,2},{4,3},{5,4},{6,5},{7,6},{9,8},{10,9},{11,10},{12... | collective-permute-start | bytes 983048 | tf_op jit(solution)/shard_map/ppermute | solution.py:18
  22.7 9.7 %copy-start.2 = (bf16[9,8,8]{0,2,1:T(8,128)(2,1)S(1)}, bf16[9,8,8]{0,2,1:T(8,128)(2,1)}, u32[]{:S(2)}) copy-start(bf16[9,8,8]{0,2,1:T(8,128)(2,1)} %param.25) | copy-start | bytes 3460
  22.7 9.8 %copy-start.7 = (bf16[64,64]{1,0:T(8,128)(2,1)S(1)}, bf16[64,64]{1,0:T(8,128)(2,1)}, u32[]{:S(2)}) copy-start(bf16[64,64]{1,0:T(8,128)(2,1)} %param.22) | copy-start | bytes 24580
  27.6 8.4 %all-to-all-start = ((bf16[4,2,8192]{2,1,0:T(2,128)(2,1)}), bf16[4,2,8192]{2,1,0:T(2,128)(2,1)S(1)}, u32[]{:S(2)}, u32[]{:S(2)}) async-start(bf16[4,2,8192]{2,1,0:T(2,128)(2,1)} %reshape.99), calls=%async_computation | async-start | bytes 262144 | tf_op jit(solution)/shard_map/all_to_all | solution.py:142
  35.0 5.1 %copy-start.3 = (bf16[64,192]{1,0:T(8,128)(2,1)S(1)}, bf16[64,192]{1,0:T(8,128)(2,1)}, u32[]{:S(2)}) copy-start(bf16[64,192]{1,0:T(8,128)(2,1)} %param.20) | copy-start | bytes 73732
  35.1 5.1 %copy-start.4 = (bf16[64,8]{0,1:T(8,128)(2,1)S(1)}, bf16[64,8]{0,1:T(8,128)(2,1)}, u32[]{:S(2)}) copy-start(bf16[64,8]{0,1:T(8,128)(2,1)} %param.23) | copy-start | bytes 3076
  35.1 5.1 %copy-start.5 = (f32[4]{0:T(128)S(1)}, f32[4]{0:T(128)}, u32[]{:S(2)}) copy-start(f32[4]{0:T(128)} %param.21) | copy-start | bytes 52
  35.1 5.1 %copy-start.6 = (bf16[8,64]{1,0:T(8,128)(2,1)S(1)}, bf16[8,64]{1,0:T(8,128)(2,1)}, u32[]{:S(2)}) copy-start(bf16[8,64]{1,0:T(8,128)(2,1)} %param.18) | copy-start | bytes 3076
  35.1 5.1 %copy-start.8 = (f32[64]{0:T(128)S(1)}, f32[64]{0:T(128)}, u32[]{:S(2)}) copy-start(f32[64]{0:T(128)} %param.19) | copy-start | bytes 772
  63.2 3.7 %copy-start = (bf16[256,4,8,8]{3,2,1,0:T(8,128)(2,1)S(1)}, bf16[256,4,8,8]{3,2,1,0:T(8,128)(2,1)}, u32[]{:S(2)}) copy-start(bf16[256,4,8,8]{3,2,1,0:T(8,128)(2,1)} %copy.211) | copy-start | bytes 393220 | tf_op jit(solution)/shard_map/while
  97.0 3.7 %copy-start = (bf16[256,4,8,8]{3,2,1,0:T(8,128)(2,1)S(1)}, bf16[256,4,8,8]{3,2,1,0:T(8,128)(2,1)}, u32[]{:S(2)}) copy-start(bf16[256,4,8,8]{3,2,1,0:T(8,128)(2,1)} %copy.211) | copy-start | bytes 393220 | tf_op jit(solution)/shard_map/while
  130.8 3.7 %copy-start = (bf16[256,4,8,8]{3,2,1,0:T(8,128)(2,1)S(1)}, bf16[256,4,8,8]{3,2,1,0:T(8,128)(2,1)}, u32[]{:S(2)}) copy-start(bf16[256,4,8,8]{3,2,1,0:T(8,128)(2,1)} %copy.211) | copy-start | bytes 393220 | tf_op jit(solution)/shard_map/while
  164.6 3.7 %copy-start = (bf16[256,4,8,8]{3,2,1,0:T(8,128)(2,1)S(1)}, bf16[256,4,8,8]{3,2,1,0:T(8,128)(2,1)}, u32[]{:S(2)}) copy-start(bf16[256,4,8,8]{3,2,1,0:T(8,128)(2,1)} %copy.211) | copy-start | bytes 393220 | tf_op jit(solution)/shard_map/while
  175.8 5.0 %collective-permute-start.2 = (bf16[8,8,8,4]{3,1,2,0:T(8,128)(2,1)S(1)}, bf16[8,8,8,4]{3,1,2,0:T(8,128)(2,1)S(1)}, u32[]{:S(2)}, u32[]{:S(2)}) collective-permute-start(bf16[8,8,8,4]{3,1,2,0:T(8,128)(2,1)S(1)} %get-tuple-element.127), channel_id=1, source_target_pairs={{0,8},{8,16},{16,24},{1,9},{9,17},{17,25},{2,10},{10,18},{18,26},{... | collective-permute-start | bytes 12296 | tf_op jit(solution)/shard_map/ppermute | solution.py:15
  178.8 6.3 %collective-permute-start.3 = (bf16[8,8,8,4]{3,1,2,0:T(8,128)(2,1)S(1)}, bf16[8,8,8,4]{3,1,2,0:T(8,128)(2,1)S(1)}, u32[]{:S(2)}, u32[]{:S(2)}) collective-permute-start(bf16[8,8,8,4]{3,1,2,0:T(8,128)(2,1)S(1)} %get-tuple-element.128), channel_id=1, source_target_pairs={{8,0},{16,8},{24,16},{9,1},{17,9},{25,17},{10,2},{18,10},{26,18},{... | collective-permute-start | bytes 12296 | tf_op jit(solution)/shard_map/ppermute | solution.py:18
  185.3 6.0 %collective-permute-start.4 = (bf16[8,8,4,136]{3,1,2,0:T(8,128)(2,1)S(1)}, bf16[8,8,4,136]{3,1,2,0:T(8,128)(2,1)S(1)}, u32[]{:S(2)}, u32[]{:S(2)}) collective-permute-start(bf16[8,8,4,136]{3,1,2,0:T(8,128)(2,1)S(1)} %get-tuple-element.123), channel_id=1, source_target_pairs={{0,1},{1,2},{2,3},{3,4},{4,5},{5,6},{6,7},{8,9},{9,10},{10,11},{11... | collective-permute-start | bytes 208904 | tf_op jit(solution)/shard_map/ppermute | solution.py:15
  189.4 6.4 %collective-permute-start.5 = (bf16[8,8,4,136]{3,1,2,0:T(8,128)(2,1)S(1)}, bf16[8,8,4,136]{3,1,2,0:T(8,128)(2,1)S(1)}, u32[]{:S(2)}, u32[]{:S(2)}) collective-permute-start(bf16[8,8,4,136]{3,1,2,0:T(8,128)(2,1)S(1)} %get-tuple-element.124), channel_id=1, source_target_pairs={{1,0},{2,1},{3,2},{4,3},{5,4},{6,5},{7,6},{9,8},{10,9},{11,10},{12... | collective-permute-start | bytes 208904 | tf_op jit(solution)/shard_map/ppermute | solution.py:18
  197.9 5.0 %collective-permute-start.6 = (bf16[8,8,8,4]{3,1,2,0:T(8,128)(2,1)S(1)}, bf16[8,8,8,4]{3,1,2,0:T(8,128)(2,1)S(1)}, u32[]{:S(2)}, u32[]{:S(2)}) collective-permute-start(bf16[8,8,8,4]{3,1,2,0:T(8,128)(2,1)S(1)} %get-tuple-element.125), channel_id=1, source_target_pairs={{0,8},{8,16},{16,24},{1,9},{9,17},{17,25},{2,10},{10,18},{18,26},{... | collective-permute-start | bytes 12296 | tf_op jit(solution)/shard_map/ppermute | solution.py:15
  200.8 6.3 %collective-permute-start.7 = (bf16[8,8,8,4]{3,1,2,0:T(8,128)(2,1)S(1)}, bf16[8,8,8,4]{3,1,2,0:T(8,128)(2,1)S(1)}, u32[]{:S(2)}, u32[]{:S(2)}) collective-permute-start(bf16[8,8,8,4]{3,1,2,0:T(8,128)(2,1)S(1)} %get-tuple-element.126), channel_id=1, source_target_pairs={{8,0},{16,8},{24,16},{9,1},{17,9},{25,17},{10,2},{18,10},{26,18},{... | collective-permute-start | bytes 12296 | tf_op jit(solution)/shard_map/ppermute | solution.py:18
  207.3 7.8 %collective-permute-start.8 = (bf16[8,8,4,136]{3,1,2,0:T(8,128)(2,1)S(1)}, bf16[8,8,4,136]{3,1,2,0:T(8,128)(2,1)S(1)}, u32[]{:S(2)}, u32[]{:S(2)}) collective-permute-start(bf16[8,8,4,136]{3,1,2,0:T(8,128)(2,1)S(1)} %get-tuple-element.121), channel_id=1, source_target_pairs={{0,1},{1,2},{2,3},{3,4},{4,5},{5,6},{6,7},{8,9},{9,10},{10,11},{11... | collective-permute-start | bytes 208904 | tf_op jit(solution)/shard_map/ppermute | solution.py:15
  211.9 5.7 %collective-permute-start.9 = (bf16[8,8,4,136]{3,1,2,0:T(8,128)(2,1)S(1)}, bf16[8,8,4,136]{3,1,2,0:T(8,128)(2,1)S(1)}, u32[]{:S(2)}, u32[]{:S(2)}) collective-permute-start(bf16[8,8,4,136]{3,1,2,0:T(8,128)(2,1)S(1)} %get-tuple-element.122), channel_id=1, source_target_pairs={{1,0},{2,1},{3,2},{4,3},{5,4},{6,5},{7,6},{9,8},{10,9},{11,10},{12... | collective-permute-start | bytes 208904 | tf_op jit(solution)/shard_map/ppermute | solution.py:18
where the time goes:
time: 221 us; the launch traced here: 220 us
  local copies, waits for them, and re-layouts  104 us (47%)
  matrix products  46 us (21%)
  starting transfers between devices  31.2 us (14%)
  waiting for transfers between devices  30 us (14%)
  other arithmetic  5.64 us (3%)
  loops' own time  3.16 us (1%)
    dot_general x4, matrix products, post_block(): jnp.einsum('pmhd,pnhd->phmn', queries, keys_all, preferred_element_type=j...  21.6 us
    ppermute x5, starting transfers between devices, padded(): lax.ppermute(lax.slice_in_dim(block, block.shape[dim] - width, None, axis...  18.5 us
    dot_general x4, matrix products, post_block(): jnp.einsum('phmn,pnhd->pmhd', probs, values, preferred_element_type=jnp.f...  16.5 us
    ppermute x5, waiting for transfers between devices, padded(): lax.ppermute(lax.slice_in_dim(block, 0, width, axis=dim), axis, backward)  15.3 us
    convert_element_type x4, local copies, waits for them, and re-layouts, post_block(): (keys_all * lax.rsqrt(jnp.sum(keys_all * keys_all, -1, keepdims=True) + 1...  15.2 us
    convert_element_type x4, local copies, waits for them, and re-layouts, post_block(): (queries * lax.rsqrt(jnp.sum(queries * queries, -1, keepdims=True) + 1.0)...  14.9 us
    reshape x4, local copies, waits for them, and re-layouts, post_block(): projected[..., 2 * width:].astype(jnp.bfloat16)  14.8 us
    convert_element_type x4, local copies, waits for them, and re-layouts, post_block(): probs = (weights / jnp.sum(weights, -1, keepdims=True)).astype(jnp.bfloat16)  14.6 us
  transfers between devices with their start and end apart: 11, of which 8 were waited for; matrix products, arithmetic and copies ran while one was open for 2% of the time, Pallas kernels for 0%

commit v1 on v0

--- a/solution.py
+++ b/solution.py
@@ -139,9 +139,9 @@
         inside = (row_ids >= 0) & (row_ids < all_rows)
         gridded_quantity_list = jnp.where(inside[None, None, :, None], gridded_quantity_list, 0.0)
     predicted_states = gridded_quantity_list.astype(jnp.bfloat16)
-    blockwise_quantity = lax.all_to_all(
-        predicted_states, "mem", split_axis=3, concat_axis=0, tiled=True
-    )
+    pieces = jnp.split(predicted_states, lax.axis_size("mem"), axis=3)
+    arrived = lax.all_to_all(jnp.stack(pieces), "mem", 0, 0)
+    blockwise_quantity = jnp.concatenate(arrived, axis=0)
     members, levels_count, tile_rows, tile_cols = blockwise_quantity.shape
     count = tile_rows * tile_cols
     flattened = blockwise_quantity.reshape(members, levels_count, count)

time: 221 us -> 213 us (0.964)
  local copies, waits for them, and re-layouts: 104 us -> 94.7 us
    unnamed x39 -> x37, local copies, waits for them, and re-layouts: 11 us -> 5.7 us
where the time goes in v1:
time: 213 us; the launch traced here: 212 us
  local copies, waits for them, and re-layouts  94.7 us (44%)
  matrix products  46.1 us (22%)
  starting transfers between devices  31.2 us (15%)
  waiting for transfers between devices  30 us (14%)
  other arithmetic  6.32 us (3%)
  loops' own time  2.98 us (1%)
    dot_general x4, matrix products, post_block(): jnp.einsum('pmhd,pnhd->phmn', queries, keys_all, preferred_element_type=j...  21.6 us
    ppermute x5, starting transfers between devices, padded(): lax.ppermute(lax.slice_in_dim(block, block.shape[dim] - width, None, axis...  18.5 us
    dot_general x4, matrix products, post_block(): jnp.einsum('phmn,pnhd->pmhd', probs, values, preferred_element_type=jnp.f...  16.5 us
    ppermute x5, waiting for transfers between devices, padded(): lax.ppermute(lax.slice_in_dim(block, 0, width, axis=dim), axis, backward)  15.3 us
    convert_element_type x4, local copies, waits for them, and re-layouts, post_block(): (keys_all * lax.rsqrt(jnp.sum(keys_all * keys_all, -1, keepdims=True) + 1...  15.3 us
    convert_element_type x4, local copies, waits for them, and re-layouts, post_block(): (queries * lax.rsqrt(jnp.sum(queries * queries, -1, keepdims=True) + 1.0)...  14.9 us
    reshape x4, local copies, waits for them, and re-layouts, post_block(): projected[..., 2 * width:].astype(jnp.bfloat16)  14.8 us
    convert_element_type x4, local copies, waits for them, and re-layouts, post_block(): probs = (weights / jnp.sum(weights, -1, keepdims=True)).astype(jnp.bfloat16)  14.6 us
  transfers between devices with their start and end apart: 11, of which 8 were waited for; matrix products, arithmetic and copies ran while one was open for 2% of the time, Pallas kernels for 0%

profile of v1, /device:TPU:1, one launch (start us, length us, event | category | flops | bytes accessed | tf_op | source)
XLA Modules:
  0.0 211.9 jit_solution(11141641986793755540)
XLA Ops:
  0.0 1.0 copy.194
  1.0 1.1 copy.117
  2.1 1.1 fusion.90
  3.4 4.0 %collective-permute-start = (f32[5,8,4,512]{3,1,2,0:T(8,128)S(1)}, f32[5,8,4,512]{3,1,2,0:T(8,128)S(1)}, u32[]{:S(2)}, u32[]{:S(2)}) collective-permute-start(f32[5,8,4,512]{3,1,2,0:T(8,128)S(1)} %get-tuple-element.115), channel_id=1, source_target_pairs={{0,1},{1,2},{2,3},{3,4},{4,5},{5,6},{6,7},{8,9},{9,10},{10,11},{11... | collective-permute-start | bytes 983048 | tf_op jit(solution)/shard_map/ppermute | solution.py:15
  7.3 1.3 collective-permute-start.1
  8.8 11.9 %collective-permute-done = f32[5,8,4,512]{3,1,2,0:T(8,128)S(1)} collective-permute-done((f32[5,8,4,512]{3,1,2,0:T(8,128)S(1)}, f32[5,8,4,512]{3,1,2,0:T(8,128)S(1)}, u32[]{:S(2)}, u32[]{:S(2)}) %collective-permute-start) | collective-permute-done | bytes 327712 | tf_op jit(solution)/shard_map/ppermute | solution.py:15
  21.0 0.5 add_select_fusion
  21.5 0.4 add_select_fusion.1
  22.8 0.7 pad_maximum_fusion.14
  23.5 4.8 %all-to-all-start = ((bf16[4,2,8,8,128]{4,2,3,1,0:T(8,128)(2,1)}), bf16[4,2,8,8,128]{4,2,3,1,0:T(8,128)(2,1)S(1)}, u32[]{:S(2)}, u32[]{:S(2)}) async-start(bf16[4,2,8,8,128]{4,2,3,1,0:T(8,128)(2,1)} %pad_maximum_fusion.14), calls=%async_computation | async-start | bytes 262144 | tf_op jit(solution)/shard_map/all_to_all | solution.py:143
  31.0 0.9 all-to-all-done
  31.9 135.3 %while.10 = (s32[]{:T(128)}, bf16[4,8,8,256]{3,2,1,0:T(8,128)(2,1)S(1)}, s32[4]{0:T(128)S(1)}, bf16[8,8,1024]{2,1,0:T(8,128)(2,1)S(1)}, bf16[8,64]{1,0:T(8,128)(...) while((s32[]{:T(128)}, ...), condition=%wide.region_5.6_spmd, body=%wide.region_0.5_spmd.sunk | while | flops 77932544 | bytes 12530179 | solution.py:162
  32.0 0.6 dynamic_slice.14
  33.5 0.4 fusion.122
  34.4 3.7 %copy.202 = bf16[256,8,4,16]{3,1,2,0:T(8,128)(2,1)} copy(bf16[256,8,4,16]{0,3,2,1:T(8,128)(2,1)S(1)} %get-tuple-element.234) | data formatting | bytes 524288 | tf_op jit(solution)/shard_map/while/body/eval_jaxpr/convert_element_type | solution.py:67
  38.1 3.8 %copy.203 = bf16[256,8,4,16]{3,1,2,0:T(8,128)(2,1)} copy(bf16[256,8,4,16]{0,3,2,1:T(8,128)(2,1)S(1)} %get-tuple-element.235) | data formatting | bytes 524288 | tf_op jit(solution)/shard_map/while/body/eval_jaxpr/convert_element_type | solution.py:70
  41.9 5.4 %fusion.123 = f32[256,4,8,8]{2,3,1,0:T(8,128)} fusion(bf16[256,8,4,16]{3,1,2,0:T(8,128)(2,1)} %copy.202, bf16[256,8,4,16]{3,1,2,0:T(8,128)(2,1)} %copy.203), kind=kOutput, calls=%fused_computation.159.clone.1 | convolution fusion | flops 2097152 | bytes 786432 | tf_op jit(solution)/shard_map/while/body/eval_jaxpr/pmhd,pnhd->phmn/dot_general | solution.py:73
  47.3 3.6 %copy.204 = f32[256,4,8,8]{0,3,2,1:T(8,128)S(1)} copy(f32[256,4,8,8]{2,3,1,0:T(8,128)} %fusion.123) | data formatting | bytes 524288 | tf_op jit(solution)/shard_map/while/body/eval_jaxpr/pmhd,pnhd->phmn/dot_general | solution.py:73
  51.2 3.7 %copy.205 = bf16[256,4,8,8]{3,2,1,0:T(8,128)(2,1)} copy(bf16[256,4,8,8]{0,3,2,1:T(8,128)(2,1)S(1)} %divide_convert_fusion.2) | data formatting | bytes 262144 | tf_op jit(solution)/shard_map/while/body/eval_jaxpr/convert_element_type | solution.py:76
  54.9 3.7 %copy.201 = bf16[256,8,4,16]{3,1,2,0:T(8,128)(2,1)} copy(bf16[256,8,4,16]{0,3,2,1:T(8,128)(2,1)S(1)} %bitcast.243) | data formatting | bytes 524288 | tf_op jit(solution)/shard_map/while/body/eval_jaxpr/reshape | solution.py:65
  58.6 4.1 %convert_bitcast_fusion.2 = bf16[256,8,4,16]{3,1,2,0:T(8,128)(2,1)} fusion(bf16[256,8,4,16]{3,1,2,0:T(8,128)(2,1)} %copy.201, bf16[256,4,8,8]{3,2,1,0:T(8,128)(2,1)S(1)} %copy-done), kind=kOutput, calls=%fused_computation.clone.1 | convolution fusion | flops 2228224 | bytes 655360 | tf_op jit(solution)/shard_map/while/body/eval_jaxpr/phmn,pnhd->pmhd/dot_general | solution.py:77
  62.7 2.7 %copy.206 = bf16[256,8,4,16]{0,3,2,1:T(8,128)(2,1)S(1)} copy(bf16[256,8,4,16]{3,1,2,0:T(8,128)(2,1)} %convert_bitcast_fusion.2) | data formatting | bytes 524288 | tf_op jit(solution)/shard_map/while/body/eval_jaxpr/convert_element_type | solution.py:78
  65.8 0.6 dynamic_slice.14
  68.2 3.7 %copy.202 = bf16[256,8,4,16]{3,1,2,0:T(8,128)(2,1)} copy(bf16[256,8,4,16]{0,3,2,1:T(8,128)(2,1)S(1)} %get-tuple-element.234) | data formatting | bytes 524288 | tf_op jit(solution)/shard_map/while/body/eval_jaxpr/convert_element_type | solution.py:67
  71.9 3.8 %copy.203 = bf16[256,8,4,16]{3,1,2,0:T(8,128)(2,1)} copy(bf16[256,8,4,16]{0,3,2,1:T(8,128)(2,1)S(1)} %get-tuple-element.235) | data formatting | bytes 524288 | tf_op jit(solution)/shard_map/while/body/eval_jaxpr/convert_element_type | solution.py:70
  75.7 5.4 %fusion.123 = f32[256,4,8,8]{2,3,1,0:T(8,128)} fusion(bf16[256,8,4,16]{3,1,2,0:T(8,128)(2,1)} %copy.202, bf16[256,8,4,16]{3,1,2,0:T(8,128)(2,1)} %copy.203), kind=kOutput, calls=%fused_computation.159.clone.1 | convolution fusion | flops 2097152 | bytes 786432 | tf_op jit(solution)/shard_map/while/body/eval_jaxpr/pmhd,pnhd->phmn/dot_general | solution.py:73
  81.1 3.6 %copy.204 = f32[256,4,8,8]{0,3,2,1:T(8,128)S(1)} copy(f32[256,4,8,8]{2,3,1,0:T(8,128)} %fusion.123) | data formatting | bytes 524288 | tf_op jit(solution)/shard_map/while/body/eval_jaxpr/pmhd,pnhd->phmn/dot_general | solution.py:73
  85.0 3.7 %copy.205 = bf16[256,4,8,8]{3,2,1,0:T(8,128)(2,1)} copy(bf16[256,4,8,8]{0,3,2,1:T(8,128)(2,1)S(1)} %divide_convert_fusion.2) | data formatting | bytes 262144 | tf_op jit(solution)/shard_map/while/body/eval_jaxpr/convert_element_type | solution.py:76
  88.7 3.7 %copy.201 = bf16[256,8,4,16]{3,1,2,0:T(8,128)(2,1)} copy(bf16[256,8,4,16]{0,3,2,1:T(8,128)(2,1)S(1)} %bitcast.243) | data formatting | bytes 524288 | tf_op jit(solution)/shard_map/while/body/eval_jaxpr/reshape | solution.py:65
  92.4 4.1 %convert_bitcast_fusion.2 = bf16[256,8,4,16]{3,1,2,0:T(8,128)(2,1)} fusion(bf16[256,8,4,16]{3,1,2,0:T(8,128)(2,1)} %copy.201, bf16[256,4,8,8]{3,2,1,0:T(8,128)(2,1)S(1)} %copy-done), kind=kOutput, calls=%fused_computation.clone.1 | convolution fusion | flops 2228224 | bytes 655360 | tf_op jit(solution)/shard_map/while/body/eval_jaxpr/phmn,pnhd->pmhd/dot_general | solution.py:77
  96.5 2.7 %copy.206 = bf16[256,8,4,16]{0,3,2,1:T(8,128)(2,1)S(1)} copy(bf16[256,8,4,16]{3,1,2,0:T(8,128)(2,1)} %convert_bitcast_fusion.2) | data formatting | bytes 524288 | tf_op jit(solution)/shard_map/while/body/eval_jaxpr/convert_element_type | solution.py:78
  99.6 0.6 dynamic_slice.14
  101.2 0.4 fusion.122
  102.0 3.7 %copy.202 = bf16[256,8,4,16]{3,1,2,0:T(8,128)(2,1)} copy(bf16[256,8,4,16]{0,3,2,1:T(8,128)(2,1)S(1)} %get-tuple-element.234) | data formatting | bytes 524288 | tf_op jit(solution)/shard_map/while/body/eval_jaxpr/convert_element_type | solution.py:67
  105.8 3.8 %copy.203 = bf16[256,8,4,16]{3,1,2,0:T(8,128)(2,1)} copy(bf16[256,8,4,16]{0,3,2,1:T(8,128)(2,1)S(1)} %get-tuple-element.235) | data formatting | bytes 524288 | tf_op jit(solution)/shard_map/while/body/eval_jaxpr/convert_element_type | solution.py:70
  109.6 5.4 %fusion.123 = f32[256,4,8,8]{2,3,1,0:T(8,128)} fusion(bf16[256,8,4,16]{3,1,2,0:T(8,128)(2,1)} %copy.202, bf16[256,8,4,16]{3,1,2,0:T(8,128)(2,1)} %copy.203), kind=kOutput, calls=%fused_computation.159.clone.1 | convolution fusion | flops 2097152 | bytes 786432 | tf_op jit(solution)/shard_map/while/body/eval_jaxpr/pmhd,pnhd->phmn/dot_general | solution.py:73
  115.0 3.6 %copy.204 = f32[256,4,8,8]{0,3,2,1:T(8,128)S(1)} copy(f32[256,4,8,8]{2,3,1,0:T(8,128)} %fusion.123) | data formatting | bytes 524288 | tf_op jit(solution)/shard_map/while/body/eval_jaxpr/pmhd,pnhd->phmn/dot_general | solution.py:73
  118.8 3.7 %copy.205 = bf16[256,4,8,8]{3,2,1,0:T(8,128)(2,1)} copy(bf16[256,4,8,8]{0,3,2,1:T(8,128)(2,1)S(1)} %divide_convert_fusion.2) | data formatting | bytes 262144 | tf_op jit(solution)/shard_map/while/body/eval_jaxpr/convert_element_type | solution.py:76
  122.5 3.7 %copy.201 = bf16[256,8,4,16]{3,1,2,0:T(8,128)(2,1)} copy(bf16[256,8,4,16]{0,3,2,1:T(8,128)(2,1)S(1)} %bitcast.243) | data formatting | bytes 524288 | tf_op jit(solution)/shard_map/while/body/eval_jaxpr/reshape | solution.py:65
  126.2 4.1 %convert_bitcast_fusion.2 = bf16[256,8,4,16]{3,1,2,0:T(8,128)(2,1)} fusion(bf16[256,8,4,16]{3,1,2,0:T(8,128)(2,1)} %copy.201, bf16[256,4,8,8]{3,2,1,0:T(8,128)(2,1)S(1)} %copy-done), kind=kOutput, calls=%fused_computation.clone.1 | convolution fusion | flops 2228224 | bytes 655360 | tf_op jit(solution)/shard_map/while/body/eval_jaxpr/phmn,pnhd->pmhd/dot_general | solution.py:77
  130.4 2.7 %copy.206 = bf16[256,8,4,16]{0,3,2,1:T(8,128)(2,1)S(1)} copy(bf16[256,8,4,16]{3,1,2,0:T(8,128)(2,1)} %convert_bitcast_fusion.2) | data formatting | bytes 524288 | tf_op jit(solution)/shard_map/while/body/eval_jaxpr/convert_element_type | solution.py:78
  133.5 0.6 dynamic_slice.14
  135.9 3.7 %copy.202 = bf16[256,8,4,16]{3,1,2,0:T(8,128)(2,1)} copy(bf16[256,8,4,16]{0,3,2,1:T(8,128)(2,1)S(1)} %get-tuple-element.234) | data formatting | bytes 524288 | tf_op jit(solution)/shard_map/while/body/eval_jaxpr/convert_element_type | solution.py:67
  139.6 3.8 %copy.203 = bf16[256,8,4,16]{3,1,2,0:T(8,128)(2,1)} copy(bf16[256,8,4,16]{0,3,2,1:T(8,128)(2,1)S(1)} %get-tuple-element.235) | data formatting | bytes 524288 | tf_op jit(solution)/shard_map/while/body/eval_jaxpr/convert_element_type | solution.py:70
  143.4 5.4 %fusion.123 = f32[256,4,8,8]{2,3,1,0:T(8,128)} fusion(bf16[256,8,4,16]{3,1,2,0:T(8,128)(2,1)} %copy.202, bf16[256,8,4,16]{3,1,2,0:T(8,128)(2,1)} %copy.203), kind=kOutput, calls=%fused_computation.159.clone.1 | convolution fusion | flops 2097152 | bytes 786432 | tf_op jit(solution)/shard_map/while/body/eval_jaxpr/pmhd,pnhd->phmn/dot_general | solution.py:73
  148.8 3.6 %copy.204 = f32[256,4,8,8]{0,3,2,1:T(8,128)S(1)} copy(f32[256,4,8,8]{2,3,1,0:T(8,128)} %fusion.123) | data formatting | bytes 524288 | tf_op jit(solution)/shard_map/while/body/eval_jaxpr/pmhd,pnhd->phmn/dot_general | solution.py:73
  152.7 3.7 %copy.205 = bf16[256,4,8,8]{3,2,1,0:T(8,128)(2,1)} copy(bf16[256,4,8,8]{0,3,2,1:T(8,128)(2,1)S(1)} %divide_convert_fusion.2) | data formatting | bytes 262144 | tf_op jit(solution)/shard_map/while/body/eval_jaxpr/convert_element_type | solution.py:76
  156.4 3.7 %copy.201 = bf16[256,8,4,16]{3,1,2,0:T(8,128)(2,1)} copy(bf16[256,8,4,16]{0,3,2,1:T(8,128)(2,1)S(1)} %bitcast.243) | data formatting | bytes 524288 | tf_op jit(solution)/shard_map/while/body/eval_jaxpr/reshape | solution.py:65
  160.1 4.1 %convert_bitcast_fusion.2 = bf16[256,8,4,16]{3,1,2,0:T(8,128)(2,1)} fusion(bf16[256,8,4,16]{3,1,2,0:T(8,128)(2,1)} %copy.201, bf16[256,4,8,8]{3,2,1,0:T(8,128)(2,1)S(1)} %copy-done), kind=kOutput, calls=%fused_computation.clone.1 | convolution fusion | flops 2228224 | bytes 655360 | tf_op jit(solution)/shard_map/while/body/eval_jaxpr/phmn,pnhd->pmhd/dot_general | solution.py:77
  164.2 2.7 %copy.206 = bf16[256,8,4,16]{0,3,2,1:T(8,128)(2,1)S(1)} copy(bf16[256,8,4,16]{3,1,2,0:T(8,128)(2,1)} %convert_bitcast_fusion.2) | data formatting | bytes 524288 | tf_op jit(solution)/shard_map/while/body/eval_jaxpr/convert_element_type | solution.py:78
  167.6 2.9 %collective-permute-start.2 = (bf16[8,8,8,4]{3,1,2,0:T(8,128)(2,1)S(1)}, bf16[8,8,8,4]{3,1,2,0:T(8,128)(2,1)S(1)}, u32[]{:S(2)}, u32[]{:S(2)}) collective-permute-start(bf16[8,8,8,4]{3,1,2,0:T(8,128)(2,1)S(1)} %get-tuple-element.127), channel_id=1, source_target_pairs={{0,8},{8,16},{16,24},{1,9},{9,17},{17,25},{2,10},{10,18},{18,26},{... | collective-permute-start | bytes 12296 | tf_op jit(solution)/shard_map/ppermute | solution.py:15
  170.5 1.9 collective-permute-start.3
  172.6 4.2 %collective-permute-done.3 = bf16[8,8,8,4]{3,1,2,0:T(8,128)(2,1)S(1)} collective-permute-done((bf16[8,8,8,4]{3,1,2,0:T(8,128)(2,1)S(1)}, bf16[8,8,8,4]{3,1,2,0:T(8,128)(2,1)S(1)}, u32[]{:S(2)}, u32[]{:S(2)}) %collective-permute-start.3) | collective-permute-done | bytes 4128 | tf_op jit(solution)/shard_map/ppermute | solution.py:18
  177.0 4.1 %collective-permute-start.4 = (bf16[8,8,4,136]{3,1,2,0:T(8,128)(2,1)S(1)}, bf16[8,8,4,136]{3,1,2,0:T(8,128)(2,1)S(1)}, u32[]{:S(2)}, u32[]{:S(2)}) collective-permute-start(bf16[8,8,4,136]{3,1,2,0:T(8,128)(2,1)S(1)} %get-tuple-element.123), channel_id=1, source_target_pairs={{0,1},{1,2},{2,3},{3,4},{4,5},{5,6},{6,7},{8,9},{9,10},{10,11},{11... | collective-permute-start | bytes 208904 | tf_op jit(solution)/shard_map/ppermute | solution.py:15
  181.1 1.5 collective-permute-start.5
  183.1 4.5 %collective-permute-done.5 = bf16[8,8,4,136]{3,1,2,0:T(8,128)(2,1)S(1)} collective-permute-done((bf16[8,8,4,136]{3,1,2,0:T(8,128)(2,1)S(1)}, bf16[8,8,4,136]{3,1,2,0:T(8,128)(2,1)S(1)}, u32[]{:S(2)}, u32[]{:S(2)}) %collective-permute-start.5) | collective-permute-done | bytes 69664 | tf_op jit(solution)/shard_map/ppermute | solution.py:18
  189.6 2.9 %collective-permute-start.6 = (bf16[8,8,8,4]{3,1,2,0:T(8,128)(2,1)S(1)}, bf16[8,8,8,4]{3,1,2,0:T(8,128)(2,1)S(1)}, u32[]{:S(2)}, u32[]{:S(2)}) collective-permute-start(bf16[8,8,8,4]{3,1,2,0:T(8,128)(2,1)S(1)} %get-tuple-element.125), channel_id=1, source_target_pairs={{0,8},{8,16},{16,24},{1,9},{9,17},{17,25},{2,10},{10,18},{18,26},{... | collective-permute-start | bytes 12296 | tf_op jit(solution)/shard_map/ppermute | solution.py:15
  192.6 1.9 collective-permute-start.7
  194.7 4.2 %collective-permute-done.7 = bf16[8,8,8,4]{3,1,2,0:T(8,128)(2,1)S(1)} collective-permute-done((bf16[8,8,8,4]{3,1,2,0:T(8,128)(2,1)S(1)}, bf16[8,8,8,4]{3,1,2,0:T(8,128)(2,1)S(1)}, u32[]{:S(2)}, u32[]{:S(2)}) %collective-permute-start.7) | collective-permute-done | bytes 4128 | tf_op jit(solution)/shard_map/ppermute | solution.py:18
  199.1 4.5 %collective-permute-start.8 = (bf16[8,8,4,136]{3,1,2,0:T(8,128)(2,1)S(1)}, bf16[8,8,4,136]{3,1,2,0:T(8,128)(2,1)S(1)}, u32[]{:S(2)}, u32[]{:S(2)}) collective-permute-start(bf16[8,8,4,136]{3,1,2,0:T(8,128)(2,1)S(1)} %get-tuple-element.121), channel_id=1, source_target_pairs={{0,1},{1,2},{2,3},{3,4},{4,5},{5,6},{6,7},{8,9},{9,10},{10,11},{11... | collective-permute-start | bytes 208904 | tf_op jit(solution)/shard_map/ppermute | solution.py:15
  203.6 1.3 collective-permute-start.9
  205.1 1.8 collective-permute-done.8
  206.9 2.4 %collective-permute-done.9 = bf16[8,8,4,136]{3,1,2,0:T(8,128)(2,1)S(1)} collective-permute-done((bf16[8,8,4,136]{3,1,2,0:T(8,128)(2,1)S(1)}, bf16[8,8,4,136]{3,1,2,0:T(8,128)(2,1)S(1)}, u32[]{:S(2)}, u32[]{:S(2)}) %collective-permute-start.9) | collective-permute-done | bytes 69664 | tf_op jit(solution)/shard_map/ppermute | solution.py:18
  211.2 0.7 copy.148
  (135 shorter events, 15.7 us)
Async XLA Ops:
  0.0 8.7 %copy-start.1 = (bf16[9,8,8]{0,2,1:T(8,128)(2,1)S(1)}, bf16[9,8,8]{0,2,1:T(8,128)(2,1)}, u32[]{:S(2)}) copy-start(bf16[9,8,8]{0,2,1:T(8,128)(2,1)} %param.24) | copy-start | bytes 3460
  3.4 17.3 %collective-permute-start = (f32[5,8,4,512]{3,1,2,0:T(8,128)S(1)}, f32[5,8,4,512]{3,1,2,0:T(8,128)S(1)}, u32[]{:S(2)}, u32[]{:S(2)}) collective-permute-start(f32[5,8,4,512]{3,1,2,0:T(8,128)S(1)} %get-tuple-element.115), channel_id=1, source_target_pairs={{0,1},{1,2},{2,3},{3,4},{4,5},{5,6},{6,7},{8,9},{9,10},{10,11},{11... | collective-permute-start | bytes 983048 | tf_op jit(solution)/shard_map/ppermute | solution.py:15
  7.3 13.4 %collective-permute-start.1 = (f32[5,8,4,512]{3,1,2,0:T(8,128)S(1)}, f32[5,8,4,512]{3,1,2,0:T(8,128)S(1)}, u32[]{:S(2)}, u32[]{:S(2)}) collective-permute-start(f32[5,8,4,512]{3,1,2,0:T(8,128)S(1)} %get-tuple-element.116), channel_id=1, source_target_pairs={{1,0},{2,1},{3,2},{4,3},{5,4},{6,5},{7,6},{9,8},{10,9},{11,10},{12... | collective-permute-start | bytes 983048 | tf_op jit(solution)/shard_map/ppermute | solution.py:18
  22.0 6.3 %copy-start.2 = (bf16[9,8,8]{0,2,1:T(8,128)(2,1)S(1)}, bf16[9,8,8]{0,2,1:T(8,128)(2,1)}, u32[]{:S(2)}) copy-start(bf16[9,8,8]{0,2,1:T(8,128)(2,1)} %param.25) | copy-start | bytes 3460
  22.0 6.4 %copy-start.7 = (bf16[64,64]{1,0:T(8,128)(2,1)S(1)}, bf16[64,64]{1,0:T(8,128)(2,1)}, u32[]{:S(2)}) copy-start(bf16[64,64]{1,0:T(8,128)(2,1)} %param.22) | copy-start | bytes 24580
  22.4 9.5 %copy-start.3 = (bf16[64,192]{1,0:T(8,128)(2,1)S(1)}, bf16[64,192]{1,0:T(8,128)(2,1)}, u32[]{:S(2)}) copy-start(bf16[64,192]{1,0:T(8,128)(2,1)} %param.20) | copy-start | bytes 73732
  22.4 9.5 %copy-start.4 = (bf16[64,8]{0,1:T(8,128)(2,1)S(1)}, bf16[64,8]{0,1:T(8,128)(2,1)}, u32[]{:S(2)}) copy-start(bf16[64,8]{0,1:T(8,128)(2,1)} %param.23) | copy-start | bytes 3076
  22.4 9.5 %copy-start.5 = (f32[4]{0:T(128)S(1)}, f32[4]{0:T(128)}, u32[]{:S(2)}) copy-start(f32[4]{0:T(128)} %param.21) | copy-start | bytes 52
  22.4 9.5 %copy-start.6 = (bf16[8,64]{1,0:T(8,128)(2,1)S(1)}, bf16[8,64]{1,0:T(8,128)(2,1)}, u32[]{:S(2)}) copy-start(bf16[8,64]{1,0:T(8,128)(2,1)} %param.18) | copy-start | bytes 3076
  22.4 9.5 %copy-start.8 = (f32[64]{0:T(128)S(1)}, f32[64]{0:T(128)}, u32[]{:S(2)}) copy-start(f32[64]{0:T(128)} %param.19) | copy-start | bytes 772
  23.5 8.4 %all-to-all-start = ((bf16[4,2,8,8,128]{4,2,3,1,0:T(8,128)(2,1)}), bf16[4,2,8,8,128]{4,2,3,1,0:T(8,128)(2,1)S(1)}, u32[]{:S(2)}, u32[]{:S(2)}) async-start(bf16[4,2,8,8,128]{4,2,3,1,0:T(8,128)(2,1)} %pad_maximum_fusion.14), calls=%async_computation | async-start | bytes 262144 | tf_op jit(solution)/shard_map/all_to_all | solution.py:143
  54.9 3.7 %copy-start = (bf16[256,4,8,8]{3,2,1,0:T(8,128)(2,1)S(1)}, bf16[256,4,8,8]{3,2,1,0:T(8,128)(2,1)}, u32[]{:S(2)}) copy-start(bf16[256,4,8,8]{3,2,1,0:T(8,128)(2,1)} %copy.205) | copy-start | bytes 393220 | tf_op jit(solution)/shard_map/while
  88.7 3.7 %copy-start = (bf16[256,4,8,8]{3,2,1,0:T(8,128)(2,1)S(1)}, bf16[256,4,8,8]{3,2,1,0:T(8,128)(2,1)}, u32[]{:S(2)}) copy-start(bf16[256,4,8,8]{3,2,1,0:T(8,128)(2,1)} %copy.205) | copy-start | bytes 393220 | tf_op jit(solution)/shard_map/while
  122.5 3.7 %copy-start = (bf16[256,4,8,8]{3,2,1,0:T(8,128)(2,1)S(1)}, bf16[256,4,8,8]{3,2,1,0:T(8,128)(2,1)}, u32[]{:S(2)}) copy-start(bf16[256,4,8,8]{3,2,1,0:T(8,128)(2,1)} %copy.205) | copy-start | bytes 393220 | tf_op jit(solution)/shard_map/while
  156.4 3.7 %copy-start = (bf16[256,4,8,8]{3,2,1,0:T(8,128)(2,1)S(1)}, bf16[256,4,8,8]{3,2,1,0:T(8,128)(2,1)}, u32[]{:S(2)}) copy-start(bf16[256,4,8,8]{3,2,1,0:T(8,128)(2,1)} %copy.205) | copy-start | bytes 393220 | tf_op jit(solution)/shard_map/while
  167.6 5.0 %collective-permute-start.2 = (bf16[8,8,8,4]{3,1,2,0:T(8,128)(2,1)S(1)}, bf16[8,8,8,4]{3,1,2,0:T(8,128)(2,1)S(1)}, u32[]{:S(2)}, u32[]{:S(2)}) collective-permute-start(bf16[8,8,8,4]{3,1,2,0:T(8,128)(2,1)S(1)} %get-tuple-element.127), channel_id=1, source_target_pairs={{0,8},{8,16},{16,24},{1,9},{9,17},{17,25},{2,10},{10,18},{18,26},{... | collective-permute-start | bytes 12296 | tf_op jit(solution)/shard_map/ppermute | solution.py:15
  170.5 6.3 %collective-permute-start.3 = (bf16[8,8,8,4]{3,1,2,0:T(8,128)(2,1)S(1)}, bf16[8,8,8,4]{3,1,2,0:T(8,128)(2,1)S(1)}, u32[]{:S(2)}, u32[]{:S(2)}) collective-permute-start(bf16[8,8,8,4]{3,1,2,0:T(8,128)(2,1)S(1)} %get-tuple-element.128), channel_id=1, source_target_pairs={{8,0},{16,8},{24,16},{9,1},{17,9},{25,17},{10,2},{18,10},{26,18},{... | collective-permute-start | bytes 12296 | tf_op jit(solution)/shard_map/ppermute | solution.py:18
  177.0 6.0 %collective-permute-start.4 = (bf16[8,8,4,136]{3,1,2,0:T(8,128)(2,1)S(1)}, bf16[8,8,4,136]{3,1,2,0:T(8,128)(2,1)S(1)}, u32[]{:S(2)}, u32[]{:S(2)}) collective-permute-start(bf16[8,8,4,136]{3,1,2,0:T(8,128)(2,1)S(1)} %get-tuple-element.123), channel_id=1, source_target_pairs={{0,1},{1,2},{2,3},{3,4},{4,5},{5,6},{6,7},{8,9},{9,10},{10,11},{11... | collective-permute-start | bytes 208904 | tf_op jit(solution)/shard_map/ppermute | solution.py:15
  181.1 6.4 %collective-permute-start.5 = (bf16[8,8,4,136]{3,1,2,0:T(8,128)(2,1)S(1)}, bf16[8,8,4,136]{3,1,2,0:T(8,128)(2,1)S(1)}, u32[]{:S(2)}, u32[]{:S(2)}) collective-permute-start(bf16[8,8,4,136]{3,1,2,0:T(8,128)(2,1)S(1)} %get-tuple-element.124), channel_id=1, source_target_pairs={{1,0},{2,1},{3,2},{4,3},{5,4},{6,5},{7,6},{9,8},{10,9},{11,10},{12... | collective-permute-start | bytes 208904 | tf_op jit(solution)/shard_map/ppermute | solution.py:18
  189.6 5.0 %collective-permute-start.6 = (bf16[8,8,8,4]{3,1,2,0:T(8,128)(2,1)S(1)}, bf16[8,8,8,4]{3,1,2,0:T(8,128)(2,1)S(1)}, u32[]{:S(2)}, u32[]{:S(2)}) collective-permute-start(bf16[8,8,8,4]{3,1,2,0:T(8,128)(2,1)S(1)} %get-tuple-element.125), channel_id=1, source_target_pairs={{0,8},{8,16},{16,24},{1,9},{9,17},{17,25},{2,10},{10,18},{18,26},{... | collective-permute-start | bytes 12296 | tf_op jit(solution)/shard_map/ppermute | solution.py:15
  192.6 6.3 %collective-permute-start.7 = (bf16[8,8,8,4]{3,1,2,0:T(8,128)(2,1)S(1)}, bf16[8,8,8,4]{3,1,2,0:T(8,128)(2,1)S(1)}, u32[]{:S(2)}, u32[]{:S(2)}) collective-permute-start(bf16[8,8,8,4]{3,1,2,0:T(8,128)(2,1)S(1)} %get-tuple-element.126), channel_id=1, source_target_pairs={{8,0},{16,8},{24,16},{9,1},{17,9},{25,17},{10,2},{18,10},{26,18},{... | collective-permute-start | bytes 12296 | tf_op jit(solution)/shard_map/ppermute | solution.py:18
  199.1 7.8 %collective-permute-start.8 = (bf16[8,8,4,136]{3,1,2,0:T(8,128)(2,1)S(1)}, bf16[8,8,4,136]{3,1,2,0:T(8,128)(2,1)S(1)}, u32[]{:S(2)}, u32[]{:S(2)}) collective-permute-start(bf16[8,8,4,136]{3,1,2,0:T(8,128)(2,1)S(1)} %get-tuple-element.121), channel_id=1, source_target_pairs={{0,1},{1,2},{2,3},{3,4},{4,5},{5,6},{6,7},{8,9},{9,10},{10,11},{11... | collective-permute-start | bytes 208904 | tf_op jit(solution)/shard_map/ppermute | solution.py:15
  203.6 5.7 %collective-permute-start.9 = (bf16[8,8,4,136]{3,1,2,0:T(8,128)(2,1)S(1)}, bf16[8,8,4,136]{3,1,2,0:T(8,128)(2,1)S(1)}, u32[]{:S(2)}, u32[]{:S(2)}) collective-permute-start(bf16[8,8,4,136]{3,1,2,0:T(8,128)(2,1)S(1)} %get-tuple-element.122), channel_id=1, source_target_pairs={{1,0},{2,1},{3,2},{4,3},{5,4},{6,5},{7,6},{9,8},{10,9},{11,10},{12... | collective-permute-start | bytes 208904 | tf_op jit(solution)/shard_map/ppermute | solution.py:18
